TPU v7x, 256 devices: a whole 4x4x8 slice. The times are simulated.
256 devices in a mesh: row: 16 (over z, core), col: 16 (over x, y).
Axes of the slice: x: 4, y: 4, z: 8, core: 2. Of those that a mesh axis runs over, the one named last changes fastest.
Arguments:
- site_tensor: bfloat16 [1024, 4, 1024], P('row', None, 'col'), may hold values from -180 to 180
- site_tangent: bfloat16 [1024, 4, 1024], P('row', None, 'col'), may hold values from -180 to 180
- left_env: bfloat16 [1024, 16384], P('row', 'col'), may hold values from -0.1875 to 0.375
- right_env: bfloat16 [1024, 16384], P('row', 'col'), may hold values from -0.046875 to 0.09375
- mpo: bfloat16 [16, 16, 4, 4], replicated, may hold values from -0.25 to 0.75
- dissipation: float32 [4], replicated, may hold values from 0.2 to 2
Outputs:
- evolved: float32 [1024, 4, 1024], P('row', None, 'col')
- evolved_tangent: float32 [1024, 4, 1024], P('row', None, 'col')
All inputs are finite; a program needn't handle non-finite values.
Results may differ from a plain program's by a relative error of at most 0.0055.
Values may be sent and summed in bfloat16 or wider, within the bound.
No kernel may reach another device: no remote copies, remote signals or barrier semaphores. Data moves between devices by JAX's collectives and lax.ppermute only.
A program may use at most 64 MiB of HBM per device.

v0:
```python
import jax
import jax.numpy as jnp
from jax import lax
from jax.sharding import PartitionSpec as P

KRYLOV = 3
taylor_order = 16


def inner(first, second):
    return jnp.sum(first * second)


def taylor(hess, dhess):
    size = hess.shape[0]
    term = jnp.zeros((size,), jnp.float32).at[0].set(1.0)
    dterm = jnp.zeros((size,), jnp.float32)
    total = term
    dtotal = dterm
    for order in range(1, taylor_order + 1):
        nterm = jnp.dot(hess, term, precision=lax.Precision.HIGHEST) / order
        dterm = (
            jnp.dot(dhess, term, precision=lax.Precision.HIGHEST)
            + jnp.dot(hess, dterm, precision=lax.Precision.HIGHEST)
        ) / order
        term = nterm
        total = total + term
        dtotal = dtotal + dterm
    return (total, dtotal)


def local(site_tensor, site_tangent, left_env, right_env, mpo, dissipation):
    rows_here, physical, cols_here = site_tensor.shape
    channels = mpo.shape[0]
    left_whole = lax.all_gather(left_env, "col", axis=1, tiled=True)
    right_whole = lax.all_gather(right_env, "row", axis=0, tiled=True)

    def apply(stacked):
        panels = stacked.shape[1]
        whole = lax.all_gather(stacked.astype(jnp.bfloat16), "row", axis=0, tiled=True)
        flat = whole.reshape(whole.shape[0], panels * physical * cols_here)
        left_three = left_whole.reshape(rows_here, flat.shape[0], channels)
        mixed = lax.dot_general(
            left_three, flat, (((1,), (0,)), ((), ())), preferred_element_type=jnp.float32
        )
        mixed = mixed.astype(jnp.bfloat16).reshape(rows_here, channels, panels, physical, cols_here)
        channel = jnp.einsum("awspr,wvpq->asqrv", mixed, mpo, preferred_element_type=jnp.float32)
        channel = channel.astype(jnp.bfloat16).reshape(
            rows_here * panels * physical, cols_here * channels
        )
        partial_rows = lax.dot_general(
            channel, right_whole, (((1,), (1,)), ((), ())), preferred_element_type=jnp.float32
        )
        partial_rows = partial_rows.reshape(rows_here, panels, physical, partial_rows.shape[1])
        summed = lax.psum_scatter(partial_rows, "col", scatter_dimension=3, tiled=True)
        return summed - dissipation[None, None, :, None] * stacked

    primal = site_tensor.astype(jnp.float32)
    tangent = site_tangent.astype(jnp.float32)
    starting = lax.psum(jnp.stack([inner(primal, primal), inner(primal, tangent)]), ("row", "col"))
    norm_site = jnp.sqrt(starting[0])
    norm_tangent = starting[1] / norm_site
    basis = [primal / norm_site]
    tangents = [(tangent - basis[0] * norm_tangent) / norm_site]
    hess = jnp.zeros((KRYLOV, KRYLOV), jnp.float32)
    dhess = jnp.zeros((KRYLOV, KRYLOV), jnp.float32)
    for level in range(KRYLOV):
        image = apply(basis[level][:, None])[:, 0]
        dimage = apply(tangents[level][:, None])[:, 0]
        counted = level + 1
        locals_list = [inner(vector, image) for vector in basis]
        locals_list = locals_list + [inner(vector, image) for vector in tangents]
        locals_list = locals_list + [inner(vector, dimage) for vector in basis]
        totals = lax.psum(jnp.stack(locals_list), ("row", "col"))
        coeffs = totals[:counted]
        across = totals[counted : 2 * counted]
        along = totals[2 * counted : 3 * counted]
        dcoeffs = across + along
        hess = hess.at[:counted, level].set(coeffs)
        dhess = dhess.at[:counted, level].set(dcoeffs)
        if level + 1 < KRYLOV:
            residual = image
            dresidual = dimage
            for index in range(counted):
                residual = residual - coeffs[index] * basis[index]
                dresidual = (
                    dresidual - dcoeffs[index] * basis[index] - coeffs[index] * tangents[index]
                )
            paired = lax.psum(
                jnp.stack([inner(residual, residual), inner(residual, dresidual)]), ("row", "col")
            )
            squared = paired[0]
            mixed_term = paired[1]
            height = jnp.sqrt(squared)
            dheight = mixed_term / height
            newvec = residual / height
            basis.append(newvec)
            tangents.append((dresidual - newvec * dheight) / height)
            hess = hess.at[level + 1, level].set(height)
            dhess = dhess.at[level + 1, level].set(dheight)
    coeff, dcoeff = taylor(hess, dhess)
    spread = jnp.zeros_like(primal)
    dspread = jnp.zeros_like(primal)
    for index in range(KRYLOV):
        spread = spread + coeff[index] * basis[index]
        dspread = dspread + coeff[index] * tangents[index] + dcoeff[index] * basis[index]
    evolved = norm_site * spread
    evolved_tangent = norm_tangent * spread + norm_site * dspread
    return (evolved, evolved_tangent)


def solution(mesh):
    in_specs = (
        P("row", None, "col"),
        P("row", None, "col"),
        P("row", "col"),
        P("row", "col"),
        P(),
        P(),
    )
    out_specs = (P("row", None, "col"), P("row", None, "col"))
    return jax.shard_map(local, mesh=mesh, in_specs=in_specs, out_specs=out_specs, check_vma=False)
```

profile of v0, /device:TPU:1, one launch (start us, length us, event | category | flops | bytes accessed | tf_op | source)
XLA Modules:
  0.0 1113.4 jit_solution(7619003044250572234)
XLA Ops:
  8.7 1.6 fusion.97
  11.6 81.9 %psum.42 = f32[2]{0:T(128)S(1)} all-reduce(f32[2]{0:T(128)S(1)} %pad_maximum_fusion), channel_id=1, replica_groups=mesh['row'=16,'col'=16] {'row','col'}, use_global_device_ids=true, to_apply=%region_2.0 | all-reduce | flops 2 | bytes 16 | tf_op jit(solution)/shard_map/psum | solution.py:60
  96.4 18.8 %all-gather = bf16[1024,4,64]{2,1,0:T(4,128)(2,1)S(1)} all-gather(bf16[64,4,64]{2,1,0:T(4,128)(2,1)S(1)} %get-tuple-element.182), channel_id=2, replica_groups=mesh['row'=16,'col'=16] {'row'}, dimensions={0}, use_global_device_ids=true | all-gather | bytes 557056 | tf_op jit(solution)/shard_map/all_gather | solution.py:40
  116.0 4.8 copy.120
  120.8 4.5 copy.122
  125.3 1.5 fusion.36
  126.9 2.0 reshape.439
  129.8 1.7 copy.125
  131.6 2.9 fusion.13
  135.4 2.1 reshape.601
  137.6 18.6 %all-gather.1 = bf16[1024,4,64]{2,1,0:T(4,128)(2,1)S(1)} all-gather(bf16[64,4,64]{2,1,0:T(4,128)(2,1)S(1)} %get-tuple-element.181), channel_id=3, replica_groups=mesh['row'=16,'col'=16] {'row'}, dimensions={0}, use_global_device_ids=true | all-gather | bytes 557056 | tf_op jit(solution)/shard_map/all_gather | solution.py:40
  157.6 1.8 fusion.37
  159.9 1.9 fusion.31
  161.8 3.6 copy.133
  165.4 2.5 fusion.16
  168.0 1.8 copy.212
  169.7 3.3 reshape.603
  173.1 37.3 %reduce-scatter.19.cloned.1.call-done = f32[64,256]{1,0:T(8,128)} async-done(((f32[1024,256]{1,0:T(8,128)}), f32[64,256]{1,0:T(8,128)}) %reduce-scatter.19.cloned.1.call-update) | async-done | bytes 65552
  211.4 80.8 %reduce-scatter.21.cloned.1.call-done = f32[64,256]{1,0:T(8,128)} async-done(((f32[1024,256]{1,0:T(8,128)}), f32[64,256]{1,0:T(8,128)}) %reduce-scatter.21.cloned.1.call-update) | async-done | bytes 65552
  294.2 2.0 pad_maximum_fusion.1
  296.1 77.2 %psum.43 = f32[3]{0:T(128)S(1)} all-reduce(f32[3]{0:T(128)S(1)} %pad_maximum_fusion.1), channel_id=1, replica_groups=mesh['row'=16,'col'=16] {'row','col'}, use_global_device_ids=true, to_apply=%region_8.0 | all-reduce | flops 3 | bytes 24 | tf_op jit(solution)/shard_map/psum | solution.py:74
  378.1 73.2 %psum.44 = f32[2]{0:T(128)S(1)} all-reduce(f32[2]{0:T(128)S(1)} %pad_maximum_fusion.2), channel_id=1, replica_groups=mesh['row'=16,'col'=16] {'row','col'}, use_global_device_ids=true, to_apply=%region_11.0 | all-reduce | flops 2 | bytes 16 | tf_op jit(solution)/shard_map/psum | solution.py:89
  453.9 18.9 %all-gather.2 = bf16[1024,4,64]{2,1,0:T(4,128)(2,1)S(1)} all-gather(bf16[64,4,64]{2,1,0:T(4,128)(2,1)S(1)} %get-tuple-element.180), channel_id=4, replica_groups=mesh['row'=16,'col'=16] {'row'}, dimensions={0}, use_global_device_ids=true | all-gather | bytes 557056 | tf_op jit(solution)/shard_map/all_gather | solution.py:40
  474.1 3.3 fusion.38
  477.5 2.0 reshape.447
  479.5 2.8 fusion.32
  482.2 3.6 copy.141
  485.9 2.5 fusion.19
  488.4 1.8 copy.214
  490.2 3.2 reshape.605
  493.5 18.4 %all-gather.3 = bf16[1024,4,64]{2,1,0:T(4,128)(2,1)S(1)} all-gather(bf16[64,4,64]{2,1,0:T(4,128)(2,1)} %get-tuple-element.173), channel_id=5, replica_groups=mesh['row'=16,'col'=16] {'row'}, dimensions={0}, use_global_device_ids=true | all-gather | bytes 557056 | tf_op jit(solution)/shard_map/all_gather | solution.py:40
  513.3 3.3 fusion.39
  516.6 2.0 reshape.450
  518.6 2.8 fusion.33
  521.4 3.6 copy.149
  525.0 2.5 fusion.22
  527.6 1.8 copy.216
  529.3 3.2 reshape.607
  532.6 33.9 %reduce-scatter.23.cloned.1.call-done = f32[64,256]{1,0:T(8,128)} async-done(((f32[1024,256]{1,0:T(8,128)}), f32[64,256]{1,0:T(8,128)}) %reduce-scatter.23.cloned.1.call-update) | async-done | bytes 65552
  567.6 80.8 %reduce-scatter.25.cloned.1.call-done = f32[64,256]{1,0:T(8,128)} async-done(((f32[1024,256]{1,0:T(8,128)}), f32[64,256]{1,0:T(8,128)}) %reduce-scatter.25.cloned.1.call-update) | async-done | bytes 65552
  650.4 3.9 stack.106
  654.3 77.2 %psum.45 = f32[6]{0:T(128)S(1)} all-reduce(f32[6]{0:T(128)S(1)} %stack.106), channel_id=1, replica_groups=mesh['row'=16,'col'=16] {'row','col'}, use_global_device_ids=true, to_apply=%region_20.0 | all-reduce | flops 6 | bytes 48 | tf_op jit(solution)/shard_map/psum | solution.py:74
  732.8 3.4 multiply_reduce_fusion.1
  737.5 73.3 %psum.46 = f32[2]{0:T(128)S(1)} all-reduce(f32[2]{0:T(128)S(1)} %pad_maximum_fusion.3), channel_id=1, replica_groups=mesh['row'=16,'col'=16] {'row','col'}, use_global_device_ids=true, to_apply=%region_23.0 | all-reduce | flops 2 | bytes 16 | tf_op jit(solution)/shard_map/psum | solution.py:89
  813.4 18.9 %all-gather.5 = bf16[1024,4,64]{2,1,0:T(4,128)(2,1)S(1)} all-gather(bf16[64,4,64]{2,1,0:T(4,128)(2,1)S(1)} %get-tuple-element.168), channel_id=7, replica_groups=mesh['row'=16,'col'=16] {'row'}, dimensions={0}, use_global_device_ids=true | all-gather | bytes 557056 | tf_op jit(solution)/shard_map/all_gather | solution.py:40
  833.7 3.3 fusion.41
  837.0 2.0 reshape.460
  839.1 2.8 fusion.35
  841.8 3.6 copy.165
  845.4 2.5 fusion.28
  848.0 1.8 copy.220
  849.7 3.2 reshape.611
  853.1 18.5 %all-gather.4 = bf16[1024,4,64]{2,1,0:T(4,128)(2,1)S(1)} all-gather(bf16[64,4,64]{2,1,0:T(4,128)(2,1)} %get-tuple-element.179), channel_id=6, replica_groups=mesh['row'=16,'col'=16] {'row'}, dimensions={0}, use_global_device_ids=true | all-gather | bytes 557056 | tf_op jit(solution)/shard_map/all_gather | solution.py:40
  872.9 3.3 fusion.40
  876.3 2.0 reshape.457
  878.3 2.8 fusion.34
  881.1 3.6 copy.157
  884.7 2.5 fusion.25
  888.2 2.1 reshape.609
  894.8 31.1 %reduce-scatter.29.cloned.1.call-done = f32[64,256]{1,0:T(8,128)} async-done(((f32[1024,256]{1,0:T(8,128)}), f32[64,256]{1,0:T(8,128)}) %reduce-scatter.29.cloned.1.call-update) | async-done | bytes 65552
  927.0 80.9 %reduce-scatter.27.cloned.1.call-done = f32[64,256]{1,0:T(8,128)} async-done(((f32[1024,256]{1,0:T(8,128)}), f32[64,256]{1,0:T(8,128)}) %reduce-scatter.27.cloned.1.call-update) | async-done | bytes 65552
  1010.3 5.8 stack.119
  1016.2 77.2 %psum.47 = f32[9]{0:T(128)S(1)} all-reduce(f32[9]{0:T(128)S(1)} %stack.119), channel_id=1, replica_groups=mesh['row'=16,'col'=16] {'row','col'}, use_global_device_ids=true, to_apply=%region_35.0 | all-reduce | flops 9 | bytes 72 | tf_op jit(solution)/shard_map/psum | solution.py:74
  1101.5 4.5 multiply_add_fusion
  (147 shorter events, 46.1 us)
Async XLA Ops:
  7.2 108.7 %copy-start.8 = (bf16[16,16,4,4]{1,3,2,0:T(4,128)(2,1)S(1)}, bf16[16,16,4,4]{1,3,2,0:T(4,128)(2,1)}, u32[]{:S(2)}) copy-start(bf16[16,16,4,4]{1,3,2,0:T(4,128)(2,1)} %param.32) | copy-start | bytes 24580
  7.2 108.9 %all-gather.9.cloned.1.call-start = ((), (), s32[]{:S(2)}) async-start(), calls=%async_computation.6 | async-start | bytes 2228224 | tf_op jit(solution)/shard_map/all_gather | solution.py:35
  7.9 123.7 %all-gather.11.cloned.1.call-start = ((), (), s32[]{:S(2)}) async-start(), calls=%async_computation.7 | async-start | bytes 2228224 | tf_op jit(solution)/shard_map/all_gather | solution.py:36
  8.7 201.7 %reduce-scatter.19.cloned.1.call-start = ((), (), s32[]{:S(2)}) async-start(), calls=%async_computation.8 | async-start | bytes 1114112
  116.0 43.8 %copy-start.9 = (bf16[16,16,4,4]{0,1,2,3:T(8,128)(2,1)}, bf16[16,16,4,4]{0,1,2,3:T(8,128)(2,1)S(1)}, u32[]{:S(2)}) copy-start(bf16[16,16,4,4]{0,1,2,3:T(8,128)(2,1)S(1)} %copy.124) | copy-start | bytes 24580
  125.3 3.6 copy-start.5
  137.6 20.1 %copy-start.6 = (bf16[64,1024,16]{1,0,2:T(8,128)(2,1)S(1)}, bf16[64,1024,16]{1,0,2:T(8,128)(2,1)}, u32[]{:S(2)}) copy-start(bf16[64,1024,16]{1,0,2:T(8,128)(2,1)} %copy-done.5) | copy-start | bytes 6291460
  137.6 154.6 %reduce-scatter.21.cloned.1.call-start = ((), (), s32[]{:S(2)}) async-start(), calls=%async_computation.9 | async-start | bytes 1114112
  159.9 5.6 copy-start
  169.7 123.6 %copy-start.1 = (bf16[64,4,64]{2,1,0:T(4,128)(2,1)S(1)}, bf16[64,4,64]{2,1,0:T(4,128)(2,1)}, u32[]{:S(2)}) copy-start(bf16[64,4,64]{2,1,0:T(4,128)(2,1)} %param.28) | copy-start | bytes 98308
  169.7 123.6 %copy-start.2 = (bf16[64,4,64]{2,1,0:T(4,128)(2,1)S(1)}, bf16[64,4,64]{2,1,0:T(4,128)(2,1)}, u32[]{:S(2)}) copy-start(bf16[64,4,64]{2,1,0:T(4,128)(2,1)} %param.29) | copy-start | bytes 98308
  169.7 123.6 %copy-start.10 = (f32[4]{0:T(128)S(1)}, f32[4]{0:T(128)}, u32[]{:S(2)}) copy-start(f32[4]{0:T(128)} %param.33) | copy-start | bytes 52
  173.0 393.5 %reduce-scatter.23.cloned.1.call-start = ((), (), s32[]{:S(2)}) async-start(), calls=%async_computation.10 | async-start | bytes 1114112
  493.4 154.9 %reduce-scatter.25.cloned.1.call-start = ((), (), s32[]{:S(2)}) async-start(), calls=%async_computation.11 | async-start | bytes 1114112
  532.6 393.4 %reduce-scatter.29.cloned.1.call-start = ((), (), s32[]{:S(2)}) async-start(), calls=%async_computation.13 | async-start | bytes 1114112
  736.2 77.2 %copy-start.3 = (f32[64,4,64]{2,1,0:T(4,128)}, f32[64,4,64]{2,1,0:T(4,128)S(1)}, u32[]{:S(2)}) copy-start(f32[64,4,64]{2,1,0:T(4,128)S(1)} %get-tuple-element.171) | copy-start | bytes 196612
  853.0 155.0 %reduce-scatter.27.cloned.1.call-start = ((), (), s32[]{:S(2)}) async-start(), calls=%async_computation.12 | async-start | bytes 1114112
  888.2 120.9 %copy-start.4 = (f32[64,4,64]{2,1,0:T(4,128)S(1)}, f32[64,4,64]{2,1,0:T(4,128)}, u32[]{:S(2)}) copy-start(f32[64,4,64]{2,1,0:T(4,128)} %copy-done.3) | copy-start | bytes 196612
  888.2 120.9 %copy-start.7 = (f32[64,4,64]{2,1,0:T(4,128)S(1)}, f32[64,4,64]{2,1,0:T(4,128)}, u32[]{:S(2)}) copy-start(f32[64,4,64]{2,1,0:T(4,128)} %get-tuple-element.169) | copy-start | bytes 196612
  890.3 203.3 %copy-start.11 = (f32[3,1]{0,1:T(1,128)S(1)}, f32[3,1]{0,1:T(1,128)}, u32[]{:S(2)}) copy-start(f32[3,1]{0,1:T(1,128)} %constant.327) | copy-start | bytes 40
Sparse Core Ops, SparseCore 0:
  10.5 52.1 all-gather.8
  64.5 40.9 all-gather.10
  137.7 72.6 reduce-scatter.18
  213.7 78.4 reduce-scatter.20
  493.6 72.8 reduce-scatter.22
  569.8 78.4 reduce-scatter.24
  853.1 72.8 reduce-scatter.28
  929.5 78.4 reduce-scatter.26
where the time goes:
time: 1120 us; the launch traced here: 1110 us
  blocking collectives  572 us (51%)
  waiting for transfers between devices  346 us (31%)
  local copies, waits for them, and re-layouts  98.9 us (9%)
  matrix products  52.6 us (5%)
  other arithmetic  22.7 us (2%)
  between operations  20.4 us (2%)
    unnamed x14, waiting for transfers between devices  346 us
    psum x3, blocking collectives, local(): totals = lax.psum(jnp.stack(locals_list), ('row', 'col'))  232 us
    psum x2, blocking collectives, local(): lax.psum(jnp.stack([inner(residual, residual), inner(residual, dresidual)...  146 us
    all_gather x6, blocking collectives, apply(): lax.all_gather(stacked.astype(jnp.bfloat16), 'row', axis=0, tiled=True)  112 us
    psum x1, blocking collectives, local(): lax.psum(jnp.stack([inner(primal, primal), inner(primal, tangent)]), ('ro...  81.9 us
    unnamed x43, local copies, waits for them, and re-layouts  31.9 us
  transfers between devices with their start and end apart: 8, of which 6 were waited for; matrix products, arithmetic and copies ran while one was open for 8% of the time, Pallas kernels for 0%

commit v1 on v0

--- a/solution.py
+++ b/solution.py
@@ -37,7 +37,24 @@
 
     def apply(stacked):
         panels = stacked.shape[1]
-        whole = lax.all_gather(stacked.astype(jnp.bfloat16), "row", axis=0, tiled=True)
+        array = stacked.astype(jnp.bfloat16)
+        count, mine, rows = (lax.axis_size("row"), lax.axis_index("row"), array.shape[0])
+        forward = [(i, (i + 1) % count) for i in range(count)]
+        left = [(i, (i - 1) % count) for i in range(count)]
+        whole = jnp.zeros((*array.shape[:0], count * rows, *array.shape[0 + 1 :]), array.dtype)
+        whole = lax.dynamic_update_slice_in_dim(whole, array, mine * rows, axis=0)
+        from_left = from_right = array
+        half = count // 2
+        for step in range(1, half + 1):
+            from_left = lax.ppermute(from_left, "row", forward)
+            whole = lax.dynamic_update_slice_in_dim(
+                whole, from_left, (mine - step) % count * rows, axis=0
+            )
+            if step < count - half:
+                from_right = lax.ppermute(from_right, "row", left)
+                whole = lax.dynamic_update_slice_in_dim(
+                    whole, from_right, (mine + step) % count * rows, axis=0
+                )
         flat = whole.reshape(whole.shape[0], panels * physical * cols_here)
         left_three = left_whole.reshape(rows_here, flat.shape[0], channels)
         mixed = lax.dot_general(

time: 1120 us -> 1220 us (1.089)
  starting transfers between devices: 0.32 us -> 159 us
  blocking collectives: 572 us -> 460 us
  local copies, waits for them, and re-layouts: 98.9 us -> 199 us
  waiting for transfers between devices: 346 us -> 293 us
    ppermute x0 -> x90, starting transfers between devices: none -> 159 us  [the longest x42 137 us: apply(): from_right = lax.ppermute(from_right, 'row', left)]
    all_gather x6 -> x0, blocking collectives: 112 us -> none  [apply(): lax.all_gather(stacked.astype(jnp.bfloat16), 'row', axis=0, tiled=True)]
    dynamic_update_slice x0 -> x96, local copies, waits for them, and re-layouts: none -> 91.9 us  [the longest x48 46 us: apply(): lax.dynamic_update_slice_in_dim(whole, from_left, (mine - step) % count *...]
    unnamed x14, waiting for transfers between devices: 346 us -> 256 us
    ppermute x0 -> x90, waiting for transfers between devices: none -> 37.5 us  [the longest x48 30.7 us: apply(): from_left = lax.ppermute(from_left, 'row', forward)]
    unnamed x43 -> x85, local copies, waits for them, and re-layouts: 31.9 us -> 47.5 us
  transfers between devices with their start and end apart: 8 -> 98, of which waited for: 6 -> 74; matrix products, arithmetic and copies ran while one was open for 8% -> 15% of each run, Pallas kernels for 0% -> 0%
where the time goes in v1:
time: 1220 us; the launch traced here: 1200 us
  blocking collectives  460 us (38%)
  waiting for transfers between devices  293 us (24%)
  local copies, waits for them, and re-layouts  199 us (16%)
  starting transfers between devices  159 us (13%)
  matrix products  50.3 us (4%)
  between operations  21.5 us (2%)
  other arithmetic  19.3 us (2%)
    unnamed x14, waiting for transfers between devices  256 us
    psum x3, blocking collectives, local(): totals = lax.psum(jnp.stack(locals_list), ('row', 'col'))  232 us
    psum x2, blocking collectives, local(): lax.psum(jnp.stack([inner(residual, residual), inner(residual, dresidual)...  146 us
    ppermute x42, starting transfers between devices, apply(): from_right = lax.ppermute(from_right, 'row', left)  137 us
    psum x1, blocking collectives, local(): lax.psum(jnp.stack([inner(primal, primal), inner(primal, tangent)]), ('ro...  81.7 us
    unnamed x85, local copies, waits for them, and re-layouts  47.5 us
    dynamic_update_slice x48, local copies, waits for them, and re-layouts, apply(): lax.dynamic_update_slice_in_dim(whole, from_left, (mine - step) % count *...  46 us
    dynamic_update_slice x42, local copies, waits for them, and re-layouts, apply(): lax.dynamic_update_slice_in_dim(whole, from_right, (mine + step) % count...  39.9 us
  transfers between devices with their start and end apart: 98, of which 74 were waited for; matrix products, arithmetic and copies ran while one was open for 15% of the time, Pallas kernels for 0%

profile of v1, /device:TPU:1, one launch (start us, length us, event | category | flops | bytes accessed | tf_op | source)
XLA Modules:
  0.0 1202.3 jit_solution(14216410660020975127)
XLA Ops:
  12.6 81.7 %psum.42 = f32[2]{0:T(128)S(1)} all-reduce(f32[2]{0:T(128)S(1)} %pad_maximum_fusion), channel_id=1, replica_groups=mesh['row'=16,'col'=16] {'row','col'}, use_global_device_ids=true, to_apply=%region_2.0 | all-reduce | flops 2 | bytes 16 | tf_op jit(solution)/shard_map/psum | solution.py:77
  108.8 3.8 collective-permute-start.22
  113.5 4.0 collective-permute-start.24
  118.4 4.0 collective-permute-start.26
  123.3 4.0 collective-permute-start.28
  139.4 4.8 copy.259
  144.2 4.5 copy.261
  155.2 2.9 fusion.16
  161.2 4.2 collective-permute-start.1
  166.3 4.0 collective-permute-start.3
  171.2 4.0 collective-permute-start.5
  176.1 4.0 collective-permute-start.7
  181.0 4.0 collective-permute-start.9
  185.9 4.0 collective-permute-start.11
  190.9 3.9 collective-permute-start.13
  215.6 3.6 copy.264
  223.5 13.1 %reshape.589 = f32[1024,256]{1,0:T(8,128)} reshape(f32[1024,1,4,64]{3,2,1,0:T(4,128)} %bitcast.725) | data formatting | bytes 2097152
  238.3 80.9 %reduce-scatter.19.cloned.1.call-done = f32[64,256]{1,0:T(8,128)} async-done(((f32[1024,256]{1,0:T(8,128)}), f32[64,256]{1,0:T(8,128)}) %reduce-scatter.19.cloned.1.call-update) | async-done | bytes 65552
  322.8 77.2 %psum.43 = f32[3]{0:T(128)S(1)} all-reduce(f32[3]{0:T(128)S(1)} %pad_maximum_fusion.1), channel_id=1, replica_groups=mesh['row'=16,'col'=16] {'row','col'}, use_global_device_ids=true, to_apply=%region_8.9 | all-reduce | flops 3 | bytes 24 | tf_op jit(solution)/shard_map/psum | solution.py:91
  404.6 73.3 %psum.44 = f32[2]{0:T(128)S(1)} all-reduce(f32[2]{0:T(128)S(1)} %pad_maximum_fusion.2), channel_id=1, replica_groups=mesh['row'=16,'col'=16] {'row','col'}, use_global_device_ids=true, to_apply=%region_11.12 | all-reduce | flops 2 | bytes 16 | tf_op jit(solution)/shard_map/psum | solution.py:106
  493.1 2.8 collective-permute-start.37
  496.8 4.0 collective-permute-start.39
  501.7 4.0 collective-permute-start.41
  506.8 3.9 collective-permute-start.43
  528.1 3.1 fusion.38
  536.1 4.0 copy.278
  544.4 3.2 reshape.593
  547.8 4.1 collective-permute-start.46
  552.8 4.0 collective-permute-start.48
  557.7 4.0 collective-permute-start.50
  562.6 4.0 collective-permute-start.52
  567.5 4.0 collective-permute-start.54
  572.4 4.2 collective-permute-start.56
  577.6 3.9 collective-permute-start.58
  598.8 3.1 fusion.39
  604.0 2.7 fusion.33
  606.7 3.6 copy.285
  614.7 3.4 reshape.595
  618.1 6.8 reduce-scatter.23.cloned.1.call-done
  625.8 80.8 %reduce-scatter.25.cloned.1.call-done = f32[64,256]{1,0:T(8,128)} async-done(((f32[1024,256]{1,0:T(8,128)}), f32[64,256]{1,0:T(8,128)}) %reduce-scatter.25.cloned.1.call-update) | async-done | bytes 65552
  708.5 3.9 stack.106
  712.4 77.2 %psum.45 = f32[6]{0:T(128)S(1)} all-reduce(f32[6]{0:T(128)S(1)} %stack.106), channel_id=1, replica_groups=mesh['row'=16,'col'=16] {'row','col'}, use_global_device_ids=true, to_apply=%region_20.21 | all-reduce | flops 6 | bytes 48 | tf_op jit(solution)/shard_map/psum | solution.py:91
  790.8 3.3 multiply_reduce_fusion.10
  795.4 73.2 %psum.46 = f32[2]{0:T(128)S(1)} all-reduce(f32[2]{0:T(128)S(1)} %pad_maximum_fusion.3), channel_id=1, replica_groups=mesh['row'=16,'col'=16] {'row','col'}, use_global_device_ids=true, to_apply=%region_23.24 | all-reduce | flops 2 | bytes 16 | tf_op jit(solution)/shard_map/psum | solution.py:106
  883.8 2.8 collective-permute-start.82
  887.6 4.0 collective-permute-start.84
  892.5 4.0 collective-permute-start.86
  897.5 3.9 collective-permute-start.88
  934.1 3.4 reshape.599
  937.6 4.1 collective-permute-start.61
  942.7 4.0 collective-permute-start.63
  947.5 4.0 collective-permute-start.65
  952.4 4.0 collective-permute-start.67
  957.3 4.0 collective-permute-start.69
  962.3 4.2 collective-permute-start.71
  967.5 3.9 collective-permute-start.73
  988.7 3.1 fusion.40
  993.9 2.8 fusion.34
  996.7 3.6 copy.292
  1010.7 4.1 reduce-scatter.29.cloned.1.call-done
  1015.7 81.0 %reduce-scatter.27.cloned.1.call-done = f32[64,256]{1,0:T(8,128)} async-done(((f32[1024,256]{1,0:T(8,128)}), f32[64,256]{1,0:T(8,128)}) %reduce-scatter.27.cloned.1.call-update) | async-done | bytes 65552
  1098.6 5.7 stack.119
  1104.5 77.2 %psum.47 = f32[9]{0:T(128)S(1)} all-reduce(f32[9]{0:T(128)S(1)} %stack.119), channel_id=1, replica_groups=mesh['row'=16,'col'=16] {'row','col'}, use_global_device_ids=true, to_apply=%region_35.36 | all-reduce | flops 9 | bytes 72 | tf_op jit(solution)/shard_map/psum | solution.py:91
  1189.7 3.8 multiply_add_fusion
  (453 shorter events, 256.0 us)
Async XLA Ops:
  7.2 132.2 %all-gather.3.cloned.1.call-start = ((), (), s32[]{:S(2)}) async-start(), calls=%async_computation.6 | async-start | bytes 2228224 | tf_op jit(solution)/shard_map/all_gather | solution.py:35
  7.9 147.3 %all-gather.5.cloned.1.call-start = ((), (), s32[]{:S(2)}) async-start(), calls=%async_computation.7 | async-start | bytes 2228224 | tf_op jit(solution)/shard_map/all_gather | solution.py:36
  8.6 228.7 %reduce-scatter.21.cloned.1.call-start = ((), (), s32[]{:S(2)}) async-start(), calls=%async_computation.9 | async-start | bytes 1114112
  103.0 4.9 collective-permute-start.19
  107.9 4.9 collective-permute-start.21
  112.8 4.9 collective-permute-start.23
  117.8 4.9 collective-permute-start.25
  118.4 4.9 collective-permute-start.26
  122.7 4.9 collective-permute-start.27
  123.3 14.7 %collective-permute-start.28 = (bf16[64,1,4,64]{0,3,2,1:T(8,128)(2,1)S(1)}, bf16[64,1,4,64]{0,3,2,1:T(8,128)(2,1)S(1)}, u32[]{:S(2)}, u32[]{:S(2)}) collective-permute-start(bf16[64,1,4,64]{0,3,2,1:T(8,128)(2,1)S(1)} %collective-permute-done.26), channel_id=1, source_target_pairs={{0,240},{16,0},{32,16},{48,32},{64,48},{80,64},{96,80},{112,96},{1... | collective-permute-start | bytes 98312 | tf_op jit(solution)/shard_map/ppermute | solution.py:54
  127.6 10.8 collective-permute-start.29
  161.1 158.0 %reduce-scatter.19.cloned.1.call-start = ((), (), s32[]{:S(2)}) async-start(), calls=%async_computation.8 | async-start | bytes 1114112
  161.2 4.9 collective-permute-start
  161.2 5.1 collective-permute-start.1
  166.1 4.9 collective-permute-start.2
  171.0 4.9 collective-permute-start.4
  171.2 4.9 collective-permute-start.5
  175.9 4.9 collective-permute-start.6
  176.1 4.9 collective-permute-start.7
  180.8 4.9 collective-permute-start.8
  181.0 4.9 collective-permute-start.9
  185.9 5.0 collective-permute-start.11
  190.6 5.0 collective-permute-start.12
  190.9 16.3 %collective-permute-start.13 = (bf16[64,1,4,64]{0,3,2,1:T(8,128)(2,1)}, bf16[64,1,4,64]{0,3,2,1:T(8,128)(2,1)}, u32[]{:S(2)}, u32[]{:S(2)}) collective-permute-start(bf16[64,1,4,64]{0,3,2,1:T(8,128)(2,1)} %collective-permute-done.11), channel_id=1, source_target_pairs={{0,240},{16,0},{32,16},{48,32},{64,48},{80,64},{96,80},{112,96},{1... | collective-permute-start | bytes 98312 | tf_op jit(solution)/shard_map/ppermute | solution.py:54
  195.7 12.7 %collective-permute-start.14 = (bf16[64,1,4,64]{0,3,2,1:T(8,128)(2,1)}, bf16[64,1,4,64]{0,3,2,1:T(8,128)(2,1)}, u32[]{:S(2)}, u32[]{:S(2)}) collective-permute-start(bf16[64,1,4,64]{0,3,2,1:T(8,128)(2,1)} %collective-permute-done.12), channel_id=1, source_target_pairs={{0,16},{16,32},{32,48},{48,64},{64,80},{80,96},{96,112},{112,128},... | collective-permute-start | bytes 98312 | tf_op jit(solution)/shard_map/ppermute | solution.py:49
  236.6 388.3 %reduce-scatter.23.cloned.1.call-start = ((), (), s32[]{:S(2)}) async-start(), calls=%async_computation.10 | async-start | bytes 1114112
  491.7 4.9 collective-permute-start.36
  496.6 4.9 collective-permute-start.38
  496.8 4.9 collective-permute-start.39
  501.5 4.9 collective-permute-start.40
  501.7 5.0 collective-permute-start.41
  506.4 5.0 collective-permute-start.42
  506.8 18.6 %collective-permute-start.43 = (bf16[64,1,4,64]{0,3,2,1:T(8,128)(2,1)}, bf16[64,1,4,64]{0,3,2,1:T(8,128)(2,1)}, u32[]{:S(2)}, u32[]{:S(2)}) collective-permute-start(bf16[64,1,4,64]{0,3,2,1:T(8,128)(2,1)} %collective-permute-done.41), channel_id=1, source_target_pairs={{0,240},{16,0},{32,16},{48,32},{64,48},{80,64},{96,80},{112,96},{1... | collective-permute-start | bytes 98312 | tf_op jit(solution)/shard_map/ppermute | solution.py:54
  511.5 14.9 %collective-permute-start.44 = (bf16[64,1,4,64]{0,3,2,1:T(8,128)(2,1)}, bf16[64,1,4,64]{0,3,2,1:T(8,128)(2,1)}, u32[]{:S(2)}, u32[]{:S(2)}) collective-permute-start(bf16[64,1,4,64]{0,3,2,1:T(8,128)(2,1)} %collective-permute-done.42), channel_id=1, source_target_pairs={{0,16},{16,32},{32,48},{48,64},{64,80},{80,96},{96,112},{112,128},... | collective-permute-start | bytes 98312 | tf_op jit(solution)/shard_map/ppermute | solution.py:49
  547.7 159.0 %reduce-scatter.25.cloned.1.call-start = ((), (), s32[]{:S(2)}) async-start(), calls=%async_computation.11 | async-start | bytes 1114112
  547.8 5.0 collective-permute-start.46
  557.5 4.9 collective-permute-start.49
  557.7 4.9 collective-permute-start.50
  562.4 4.9 collective-permute-start.51
  562.6 4.9 collective-permute-start.52
  567.3 4.9 collective-permute-start.53
  567.5 4.9 collective-permute-start.54
  572.2 4.9 collective-permute-start.55
  572.4 5.2 collective-permute-start.56
  577.1 5.0 collective-permute-start.57
  577.6 18.4 %collective-permute-start.58 = (bf16[64,1,4,64]{0,3,2,1:T(8,128)(2,1)}, bf16[64,1,4,64]{0,3,2,1:T(8,128)(2,1)}, u32[]{:S(2)}, u32[]{:S(2)}) collective-permute-start(bf16[64,1,4,64]{0,3,2,1:T(8,128)(2,1)} %collective-permute-done.56), channel_id=1, source_target_pairs={{0,240},{16,0},{32,16},{48,32},{64,48},{80,64},{96,80},{112,96},{1... | collective-permute-start | bytes 98312 | tf_op jit(solution)/shard_map/ppermute | solution.py:54
  582.2 14.9 %collective-permute-start.59 = (bf16[64,1,4,64]{0,3,2,1:T(8,128)(2,1)}, bf16[64,1,4,64]{0,3,2,1:T(8,128)(2,1)}, u32[]{:S(2)}, u32[]{:S(2)}) collective-permute-start(bf16[64,1,4,64]{0,3,2,1:T(8,128)(2,1)} %collective-permute-done.57), channel_id=1, source_target_pairs={{0,16},{16,32},{32,48},{48,64},{64,80},{80,96},{96,112},{112,128},... | collective-permute-start | bytes 98312 | tf_op jit(solution)/shard_map/ppermute | solution.py:49
  618.1 396.7 %reduce-scatter.29.cloned.1.call-start = ((), (), s32[]{:S(2)}) async-start(), calls=%async_computation.13 | async-start | bytes 1114112
  882.5 4.9 collective-permute-start.81
  887.4 4.9 collective-permute-start.83
  887.6 4.9 collective-permute-start.84
  892.3 4.9 collective-permute-start.85
  892.5 5.0 collective-permute-start.86
  897.2 5.0 collective-permute-start.87
  897.5 20.1 %collective-permute-start.88 = (bf16[64,1,4,64]{0,3,2,1:T(8,128)(2,1)}, bf16[64,1,4,64]{0,3,2,1:T(8,128)(2,1)}, u32[]{:S(2)}, u32[]{:S(2)}) collective-permute-start(bf16[64,1,4,64]{0,3,2,1:T(8,128)(2,1)} %collective-permute-done.86), channel_id=1, source_target_pairs={{0,240},{16,0},{32,16},{48,32},{64,48},{80,64},{96,80},{112,96},{1... | collective-permute-start | bytes 98312 | tf_op jit(solution)/shard_map/ppermute | solution.py:54
  902.3 16.4 %collective-permute-start.89 = (bf16[64,1,4,64]{0,3,2,1:T(8,128)(2,1)}, bf16[64,1,4,64]{0,3,2,1:T(8,128)(2,1)}, u32[]{:S(2)}, u32[]{:S(2)}) collective-permute-start(bf16[64,1,4,64]{0,3,2,1:T(8,128)(2,1)} %collective-permute-done.87), channel_id=1, source_target_pairs={{0,16},{16,32},{32,48},{48,64},{64,80},{80,96},{96,112},{112,128},... | collective-permute-start | bytes 98312 | tf_op jit(solution)/shard_map/ppermute | solution.py:49
  937.5 159.2 %reduce-scatter.27.cloned.1.call-start = ((), (), s32[]{:S(2)}) async-start(), calls=%async_computation.12 | async-start | bytes 1114112
  937.6 5.0 collective-permute-start.61
  947.4 4.9 collective-permute-start.64
  957.3 4.9 collective-permute-start.69
  962.3 5.2 collective-permute-start.71
  967.0 5.0 collective-permute-start.72
  967.5 18.4 %collective-permute-start.73 = (bf16[64,1,4,64]{0,3,2,1:T(8,128)(2,1)}, bf16[64,1,4,64]{0,3,2,1:T(8,128)(2,1)}, u32[]{:S(2)}, u32[]{:S(2)}) collective-permute-start(bf16[64,1,4,64]{0,3,2,1:T(8,128)(2,1)} %collective-permute-done.71), channel_id=1, source_target_pairs={{0,240},{16,0},{32,16},{48,32},{64,48},{80,64},{96,80},{112,96},{1... | collective-permute-start | bytes 98312 | tf_op jit(solution)/shard_map/ppermute | solution.py:54
  972.0 14.9 %collective-permute-start.74 = (bf16[64,1,4,64]{0,3,2,1:T(8,128)(2,1)}, bf16[64,1,4,64]{0,3,2,1:T(8,128)(2,1)}, u32[]{:S(2)}, u32[]{:S(2)}) collective-permute-start(bf16[64,1,4,64]{0,3,2,1:T(8,128)(2,1)} %collective-permute-done.72), channel_id=1, source_target_pairs={{0,16},{16,32},{32,48},{48,64},{64,80},{80,96},{96,112},{112,128},... | collective-permute-start | bytes 98312 | tf_op jit(solution)/shard_map/ppermute | solution.py:49
  (65 other events, 1080.1 us)
Sparse Core Ops, SparseCore 0:
  10.5 52.2 all-gather.2
  64.5 40.7 all-gather.4
  161.3 75.9 reduce-scatter.20
  240.7 78.4 reduce-scatter.18
  547.8 77.0 reduce-scatter.22
  628.2 78.3 reduce-scatter.24
  937.7 77.0 reduce-scatter.28
  1018.3 78.3 reduce-scatter.26
